TPU v7x, 512 devices: a whole 4x8x8 slice. The times are simulated.
512 devices in a mesh: row: 32 (over z_hi, x, core), col: 16 (over z_lo, y).
Axes of the slice: x: 4, y: 8, z: 8 (z_hi: 4, z_lo: 2; z = z_hi * 2 + z_lo), core: 2. Of those that a mesh axis runs over, the one named last changes fastest.
Arguments:
- amps: float32 [32, 4, 576, 576], P(None, None, 'row', 'col'), may hold values from -6 to 6
- integrals: float32 [4, 576, 32, 576], P(None, 'row', 'col'), may hold values from -0.5 to 0.5
- e_occ: float32 [32], replicated, may hold values from -2 to -0.5
- e_vir: float32 [576], replicated, may hold values from 0.5 to 3
Outputs:
- update: float32 [32, 32, 576, 576], P('row', 'col')
All inputs are finite; a program needn't handle non-finite values.
Results may differ from a plain program's by a relative error of at most 0.00007.
Values sent between devices are 32-bit elements; how exact they have to be, the bound alone decides.
No kernel may reach another device: no remote copies, remote signals or barrier semaphores. Data moves between devices by JAX's collectives and lax.ppermute only.
A program may use at most 128 MiB of HBM per device.

v0:
```python
import jax
import jax.numpy as jnp
from jax import lax
from jax.sharding import PartitionSpec as P


def contract(left, right):
    return jnp.einsum(
        "ikac,kcjb->ijab",
        left,
        right,
        precision=lax.Precision.HIGHEST,
        preferred_element_type=jnp.float32,
    )


def shards(amps, integrals, e_occ, e_vir):
    row_count = lax.axis_size("row")
    col_count = lax.axis_size("col")
    row_index = lax.axis_index("row")
    col_index = lax.axis_index("col")
    occ_col = e_occ.shape[0] // col_count
    vir_row = e_vir.shape[0] // row_count
    a_energy = lax.dynamic_slice_in_dim(e_vir, row_index * vir_row, vir_row)
    j_energy = lax.dynamic_slice_in_dim(e_occ, col_index * occ_col, occ_col)
    gathered = lax.all_gather(integrals, "row", axis=1, tiled=True)
    contracted = contract(lax.all_gather(amps, "col", axis=3, tiled=True), gathered)
    denom = (
        e_occ[:, None, None, None]
        + j_energy[None, :, None, None]
        - a_energy[None, None, :, None]
        - e_vir[None, None, None, :]
    )
    scaled = contracted / denom
    scaled = lax.all_to_all(scaled, "row", split_axis=0, concat_axis=2, tiled=True)
    return scaled


def solution(mesh):
    placed = (P(None, None, "row", "col"), P(None, "row", "col", None), P(), P())
    return jax.shard_map(
        shards, mesh=mesh, in_specs=placed, out_specs=P("row", "col", None, None), check_vma=False
    )
```

profile of v0, /device:TPU:1, one launch (start us, length us, event | category | flops | bytes accessed | tf_op | source)
XLA Modules:
  0.0 468.0 jit_solution(11950487437803002496)
XLA Ops:
  6.5 0.0 copy-start
  6.5 0.0 copy-start.2
  6.5 0.0 copy-start.1
  6.5 0.0 all-gather.5.cloned.1.call-start
  6.5 2.6 copy.19
  9.2 0.0 all-gather.5.cloned.1.call-update
  9.2 0.0 all-gather.3.cloned.1.call-start
  9.3 0.0 copy-done
  9.3 0.8 copy.18
  10.1 0.0 all-gather.3.cloned.1.call-update
  10.1 0.0 copy-done.2
  10.1 0.1 dynamic_slice.7
  10.2 0.0 copy-done.1
  10.2 0.1 dynamic_slice.6
  10.3 0.1 broadcast_add_fusion
  10.4 0.1 broadcast_subtract_fusion
  10.4 237.1 %all-gather.5.cloned.1.call-done = f32[32,4,18,576]{0,1,2,3:T(4,128)} async-done(((f32[32,4,18,36]{0,1,2,3:T(4,128)}), f32[32,4,18,576]{0,1,2,3:T(4,128)}) %all-gather.5.cloned.1.call-update) | async-done | bytes 5308432 | tf_op jit(solution)/shard_map/all_gather | solution.py:27
  247.5 18.0 %copy.21 = f32[32,4,18,576]{3,0,1,2:T(8,128)} copy(f32[32,4,18,576]{0,1,2,3:T(4,128)} %all-gather.5.cloned.1.call-done) | data formatting | bytes 10616832 | tf_op jit(solution)/shard_map/all_gather | solution.py:27
  265.5 84.8 %all-gather.3.cloned.1.call-done = f32[4,576,2,576]{3,0,2,1:T(4,128)} async-done(((f32[4,18,2,576]{3,0,2,1:T(4,128)}), f32[4,576,2,576]{3,0,2,1:T(4,128)}) %all-gather.3.cloned.1.call-update) | async-done | bytes 10616848 | tf_op jit(solution)/shard_map/all_gather | solution.py:26
  350.2 31.1 %bitcast_divide_fusion = f32[32,2,18,576]{3,0,2,1:T(8,128)S(1)} fusion(f32[32,4,18,576]{3,0,1,2:T(8,128)} %copy.21, f32[4,576,2,576,1]{3,0,2,1,4:T(4,128)} %bitcast.17, f32[576]{0:T(1024)S(1)} %copy-done.2, f32[32,2,18]{0,2,1:T(8,128)S(1)} %broadcast_subtract_fusion), kind=kOutput, calls=%fused_computation.3 | convolution fusion | flops 18347212800 | bytes 18586368 | tf_op jit(solution)/shard_map/ikac,kcjb->ijab/dot_general | solution.py:8
  381.4 2.3 copy.22
  383.7 75.7 %all_to_all.18 = f32[32,2,18,576]{3,1,2,0:T(2,128)S(1)} all-to-all(f32[32,2,18,576]{3,1,2,0:T(2,128)S(1)} %copy.22), channel_id=1, replica_groups=mesh['row'=32,'col'=16] {'row'}, dimensions={0} | all-to-all | bytes 5308416 | tf_op jit(solution)/shard_map/all_to_all | solution.py:35
  459.3 1.8 copy.23
Async XLA Ops:
  6.5 2.7 copy-start
  6.5 3.6 copy-start.2
  6.5 3.7 copy-start.1
  6.5 241.0 %all-gather.5.cloned.1.call-start = ((), (), s32[]{:S(2)}) async-start(), calls=%async_computation.2 | async-start | bytes 22560768 | tf_op jit(solution)/shard_map/all_gather | solution.py:27
  9.2 341.0 %all-gather.3.cloned.1.call-start = ((), (), s32[]{:S(2)}) async-start(), calls=%async_computation.1 | async-start | bytes 12165120 | tf_op jit(solution)/shard_map/all_gather | solution.py:26
Sparse Core Ops, SparseCore 0:
  9.4 238.0 all-gather.4
  250.6 99.5 all-gather.2
where the time goes:
time: 469 us; the launch traced here: 468 us
  waiting for transfers between devices  322 us (69%)
  blocking collectives  75.7 us (16%)
  matrix products  31.1 us (7%)
  local copies, waits for them, and re-layouts  25.7 us (5%)
  between operations  13.4 us (3%)
    all_gather x1, waiting for transfers between devices, shards(): lax.all_gather(amps, 'col', axis=3, tiled=True)  237 us
    all_gather x1, waiting for transfers between devices, shards(): gathered = lax.all_gather(integrals, 'row', axis=1, tiled=True)  84.8 us
    all_to_all x1, blocking collectives, shards(): lax.all_to_all(scaled, 'row', split_axis=0, concat_axis=2, tiled=True)  75.7 us
    dot_general x1, matrix products, contract(): jnp.einsum('ikac,kcjb->ijab', left, right, precision=lax.Precision.HIGHES...  31.1 us
    all_gather x1, local copies, waits for them, and re-layouts, shards(): lax.all_gather(amps, 'col', axis=3, tiled=True)  18 us
  transfers between devices with their start and end apart: 2, of which 2 were waited for; matrix products, arithmetic and copies ran while one was open for 4% of the time, Pallas kernels for 0%

commit v1 on v0

--- a/solution.py
+++ b/solution.py
@@ -23,7 +23,9 @@
     vir_row = e_vir.shape[0] // row_count
     a_energy = lax.dynamic_slice_in_dim(e_vir, row_index * vir_row, vir_row)
     j_energy = lax.dynamic_slice_in_dim(e_occ, col_index * occ_col, occ_col)
-    gathered = lax.all_gather(integrals, "row", axis=1, tiled=True)
+    gathered = jnp.concatenate(
+        lax.all_to_all(jnp.stack([integrals] * lax.axis_size("row")), "row", 0, 0), axis=1
+    )
     contracted = contract(lax.all_gather(amps, "col", axis=3, tiled=True), gathered)
     denom = (
         e_occ[:, None, None, None]

time: 469 us -> 622 us (1.33)
  waiting for transfers between devices: 322 us -> 455 us
  starting transfers between devices: 0.04 us -> 14.7 us
  local copies, waits for them, and re-layouts: 25.7 us -> 36.9 us
    all_to_all x0 -> x1, waiting for transfers between devices: none -> 165 us  [shards(): lax.all_to_all(jnp.stack([integrals] * lax.axis_size('row')), 'row', 0, 0)]
    all_gather x1 -> x0, waiting for transfers between devices: 84.8 us -> none  [shards(): gathered = lax.all_gather(integrals, 'row', axis=1, tiled=True)]
    all_gather x1, waiting for transfers between devices: 237 us -> 290 us  [shards(): lax.all_gather(amps, 'col', axis=3, tiled=True)]
    all_to_all x0 -> x1, starting transfers between devices: none -> 14.6 us  [shards(): lax.all_to_all(jnp.stack([integrals] * lax.axis_size('row')), 'row', 0, 0)]
    reshape x0 -> x1, local copies, waits for them, and re-layouts: none -> 7.64 us  [shards(): jnp.concatenate(lax.all_to_all(jnp.stack([integrals] * lax.axis_size('row...]
  transfers between devices with their start and end apart: 2 -> 2, of which waited for: 2 -> 2; matrix products, arithmetic and copies ran while one was open for 4% -> 3% of each run, Pallas kernels for 0% -> 0%
where the time goes in v1:
time: 622 us; the launch traced here: 619 us
  waiting for transfers between devices  455 us (73%)
  blocking collectives  70.9 us (11%)
  local copies, waits for them, and re-layouts  36.9 us (6%)
  matrix products  28.5 us (5%)
  starting transfers between devices  14.7 us (2%)
  between operations  13.5 us (2%)
    all_gather x1, waiting for transfers between devices, shards(): lax.all_gather(amps, 'col', axis=3, tiled=True)  290 us
    all_to_all x1, waiting for transfers between devices, shards(): lax.all_to_all(jnp.stack([integrals] * lax.axis_size('row')), 'row', 0, 0)  165 us
    all_to_all x1, blocking collectives, shards(): lax.all_to_all(scaled, 'row', split_axis=0, concat_axis=2, tiled=True)  70.9 us
    dot_general x1, matrix products, contract(): jnp.einsum('ikac,kcjb->ijab', left, right, precision=lax.Precision.HIGHES...  28.5 us
    all_gather x1, local copies, waits for them, and re-layouts, shards(): lax.all_gather(amps, 'col', axis=3, tiled=True)  17.9 us
    all_to_all x1, starting transfers between devices, shards(): lax.all_to_all(jnp.stack([integrals] * lax.axis_size('row')), 'row', 0, 0)  14.6 us
  transfers between devices with their start and end apart: 2, of which 2 were waited for; matrix products, arithmetic and copies ran while one was open for 3% of the time, Pallas kernels for 0%

profile of v1, /device:TPU:1, one launch (start us, length us, event | category | flops | bytes accessed | tf_op | source)
XLA Modules:
  0.0 619.2 jit_solution(17316195836790806024)
XLA Ops:
  6.5 5.5 stack.2
  12.0 0.0 copy-start.1
  12.0 0.0 copy-start.3
  12.0 0.0 copy-start.2
  12.0 14.6 %all-to-all-start = ((f32[32,4,18,2,576]{4,3,2,1,0:T(2,128)}), f32[32,4,18,2,576]{4,3,2,1,0:T(2,128)}, u32[]{:S(2)}, u32[]{:S(2)}) async-start(f32[32,4,18,2,576]{4,3,2,1,0:T(2,128)} %stack.2), calls=%async_computation | async-start | bytes 23592960 | tf_op jit(solution)/shard_map/all_to_all | solution.py:27
  26.7 0.0 all-gather.2.cloned.1.call-start
  26.7 0.0 copy-done.1
  26.7 1.6 copy.19
  28.4 0.0 all-gather.2.cloned.1.call-update
  28.4 0.0 copy-done.3
  28.4 0.1 dynamic_slice.7
  28.5 0.0 copy-done.2
  28.5 0.1 dynamic_slice.6
  28.6 0.1 broadcast_add_fusion
  28.6 0.1 broadcast_subtract_fusion
  28.7 289.9 %all-gather.2.cloned.1.call-done = f32[32,4,18,576]{0,1,2,3:T(4,128)} async-done(((f32[32,4,18,36]{0,1,2,3:T(4,128)}), f32[32,4,18,576]{0,1,2,3:T(4,128)}) %all-gather.2.cloned.1.call-update) | async-done | bytes 5308432 | tf_op jit(solution)/shard_map/all_gather | solution.py:29
  318.6 17.9 %copy.21 = f32[32,4,18,576]{3,0,1,2:T(8,128)} copy(f32[32,4,18,576]{0,1,2,3:T(4,128)} %all-gather.2.cloned.1.call-done) | data formatting | bytes 10616832 | tf_op jit(solution)/shard_map/all_gather | solution.py:29
  336.5 164.7 %all-to-all-done = f32[32,4,18,2,576]{4,3,2,1,0:T(2,128)} async-done(((f32[32,4,18,2,576]{4,3,2,1,0:T(2,128)}), f32[32,4,18,2,576]{4,3,2,1,0:T(2,128)}, u32[]{:S(2)}, u32[]{:S(2)}) %all-to-all-start) | async-done | bytes 10616864 | tf_op jit(solution)/shard_map/all_to_all | solution.py:27
  501.2 7.6 %copy.18 = f32[4,32,18,2,576]{4,3,2,1,0:T(2,128)S(1)} copy(f32[4,32,18,2,576]{4,3,2,0,1:T(2,128)} %bitcast) | data formatting | bytes 21233664 | tf_op jit(solution)/shard_map/reshape | solution.py:26
  508.8 0.0 copy-done
  508.9 28.5 %bitcast_divide_fusion = f32[32,2,18,576]{3,0,2,1:T(8,128)S(1)} fusion(f32[32,4,18,576]{3,0,1,2:T(8,128)S(1)} %copy-done, f32[4,576,2,576,1]{3,2,1,0,4:T(2,128)S(1)} %bitcast.19, f32[576]{0:T(1024)S(1)} %copy-done.3, f32[32,2,18]{0,2,1:T(8,128)S(1)} %broadcast_subtract_fusion), kind=kOutput, calls=%fused_computation.3 | convolution fusion | flops 18347212800 | bytes 18586368 | tf_op jit(solution)/shard_map/ikac,kcjb->ijab/dot_general | solution.py:8
  537.4 2.3 copy.22
  539.7 70.9 %all_to_all.23 = f32[32,2,18,576]{3,1,2,0:T(2,128)S(1)} all-to-all(f32[32,2,18,576]{3,1,2,0:T(2,128)S(1)} %copy.22), channel_id=1, replica_groups=mesh['row'=32,'col'=16] {'row'}, dimensions={0} | all-to-all | bytes 5308416 | tf_op jit(solution)/shard_map/all_to_all | solution.py:37
  610.6 1.8 copy.23
  (1 shorter events, 0.0 us)
Async XLA Ops:
  12.0 14.7 %copy-start.1 = (f32[32,4,18,36]{3,1,2,0:T(4,128)S(1)}, f32[32,4,18,36]{3,1,2,0:T(4,128)}, u32[]{:S(2)}) copy-start(f32[32,4,18,36]{3,1,2,0:T(4,128)} %param.4) | copy-start | bytes 995332
  12.0 16.4 %copy-start.3 = (f32[576]{0:T(1024)S(1)}, f32[576]{0:T(1024)}, u32[]{:S(2)}) copy-start(f32[576]{0:T(1024)} %param.7) | copy-start | bytes 6916
  12.0 16.4 %copy-start.2 = (f32[32]{0:T(128)S(1)}, f32[32]{0:T(128)}, u32[]{:S(2)}) copy-start(f32[32]{0:T(128)} %param.6) | copy-start | bytes 388
  12.0 489.1 %all-to-all-start = ((f32[32,4,18,2,576]{4,3,2,1,0:T(2,128)}), f32[32,4,18,2,576]{4,3,2,1,0:T(2,128)}, u32[]{:S(2)}, u32[]{:S(2)}) async-start(f32[32,4,18,2,576]{4,3,2,1,0:T(2,128)} %stack.2), calls=%async_computation | async-start | bytes 23592960 | tf_op jit(solution)/shard_map/all_to_all | solution.py:27
  26.7 291.9 %all-gather.2.cloned.1.call-start = ((), (), s32[]{:S(2)}) async-start(), calls=%async_computation.2 | async-start | bytes 22560768 | tf_op jit(solution)/shard_map/all_gather | solution.py:29
  501.2 7.7 %copy-start = (f32[32,4,18,576]{3,0,1,2:T(8,128)S(1)}, f32[32,4,18,576]{3,0,1,2:T(8,128)}, u32[]{:S(2)}) copy-start(f32[32,4,18,576]{3,0,1,2:T(8,128)} %copy.21) | copy-start | bytes 15925252
Sparse Core Ops, SparseCore 0:
  29.6 288.9 all-gather.1
